TPU v7x, 32 devices: a whole 2x2x4 slice. The times are simulated.
32 devices in a mesh: pages: 8 (over y, x, core), mp: 4 (over z).
Axes of the slice: x: 2, y: 2, z: 4, core: 2. Of those that a mesh axis runs over, the one named last changes fastest.
Arguments:
- hidden_in: bfloat16 [2048, 1280], P('pages'), may hold values from -240 to 240
- w_qkv: bfloat16 [3, 1280, 1280], P(None, None, 'mp'), may hold values from -0.15625 to 0.15625
- w_out: bfloat16 [1280, 1280], replicated, may hold values from -0.15625 to 0.15625
- w_gate_up: bfloat16 [2, 1280, 5120], P(None, None, 'mp'), may hold values from -0.15625 to 0.15625
- w_down: bfloat16 [5120, 1280], P('mp'), may hold values from -0.078125 to 0.078125
- scale_qk: float32 [1280], replicated, may hold values from 0.4 to 1.6
- scale_gate_up: float32 [2, 5120], P(None, 'mp'), may hold values from 0.5 to 2
- eigen_rates: float32 [2, 1280], replicated, may hold values from 0.1 to 1
- cache_keys: bfloat16 [32, 128, 1280], P('pages'), may hold values from -6 to 6
- cache_values: bfloat16 [32, 128, 1280], P('pages'), may hold values from -6 to 6
- page_table: int32 [32], replicated, may hold values from 0 to 31, as said below
- request_group: int32 [8, 4], replicated, may hold values from 0 to 7
- suffix_len: int32 [8, 4], replicated, may hold values from 1 to 253, as said below
Outputs:
- hidden_out: bfloat16 [2048, 1280], P(('pages', 'mp'))
Inputs may be any that keep to these rules, and one draw needn't show every extreme that they name: `suffix_len`: the 4 lengths of one index of pages sum to at least 153 and at most 256, and to exactly 256 for at least one index. `page_table`: A permutation of the pool pages; the 4 pool pages of one index of pages hold prefix pages of 4 different groups.
All inputs are finite; a program needn't handle non-finite values.
Results may differ from a plain program's by a relative error of at most 0.013.
Values may be sent and summed in bfloat16 or wider, within the bound.
No kernel may reach another device: no remote copies, remote signals or barrier semaphores. Data moves between devices by JAX's collectives and lax.ppermute only.
A program may use at most 128 MiB of HBM per device.

v0:
```python
import math
import jax
import jax.numpy as jnp
from jax import lax
from jax.sharding import PartitionSpec as P

HEADS = 20
GROUPS = 8
EPSILON = 1e-06


def rms_rows(values_in):
    return values_in * lax.rsqrt(jnp.mean(values_in * values_in, axis=-1, keepdims=True) + EPSILON)


def head_norm(values_in, scale_vec, head_count):
    row_count, model_width = values_in.shape
    per_head = values_in.reshape(row_count, head_count, model_width // head_count)
    normed = per_head * lax.rsqrt(jnp.mean(per_head * per_head, axis=-1, keepdims=True) + EPSILON)
    return normed.reshape(row_count, model_width) * scale_vec[None, :]


def rotate(values_in, position, head_count):
    row_count, model_width = values_in.shape
    head_dim = model_width // head_count
    half_dim = head_dim // 2
    frequency = jnp.exp(
        jnp.arange(half_dim).astype(jnp.float32) * (-2.0 * math.log(10000.0) / head_dim)
    )
    rotation = position.astype(jnp.float32)[:, None] * frequency[None, :]
    cosine_table = jnp.cos(rotation)[:, None, :]
    sine_table = jnp.sin(rotation)[:, None, :]
    per_head = values_in.reshape(row_count, head_count, head_dim)
    lower_half = per_head[:, :, :half_dim]
    upper_half = per_head[:, :, half_dim:]
    turned = jnp.concatenate(
        [
            lower_half * cosine_table - upper_half * sine_table,
            upper_half * cosine_table + lower_half * sine_table,
        ],
        axis=-1,
    )
    return turned.reshape(row_count, model_width)


def slot_tables(suffix_len, request_group, slot_count):
    end_slots = jnp.cumsum(suffix_len, axis=1)
    start_slots = end_slots - suffix_len
    slot_ids = jnp.arange(slot_count)
    inside = (slot_ids[None, None, :] >= start_slots[:, :, None]) & (
        slot_ids[None, None, :] < end_slots[:, :, None]
    )
    request_ids = jnp.arange(suffix_len.shape[1])
    slot_valid = jnp.any(inside, axis=1)
    request = jnp.sum(jnp.where(inside, request_ids[None, :, None], 0), axis=1)
    offset = slot_ids[None, :] - jnp.sum(jnp.where(inside, start_slots[:, :, None], 0), axis=1)
    group_id = jnp.where(
        slot_valid, jnp.sum(jnp.where(inside, request_group[:, :, None], 0), axis=1), -1
    )
    return (slot_valid, request, offset, group_id)


def prefix_block(query_block, group_block, prefix_keys, prefix_values, key_group, score_scale):
    row_count, model_width = query_block.shape
    head_dim = model_width // HEADS
    query_heads = query_block.reshape(row_count, HEADS, head_dim)
    key_heads = prefix_keys.reshape(-1, HEADS, head_dim)
    value_heads = prefix_values.reshape(-1, HEADS, head_dim)
    scores = (
        jnp.einsum("qhd,khd->qhk", query_heads, key_heads, preferred_element_type=jnp.float32)
        * score_scale
    )
    allowed = group_block[:, None] == key_group[None, :]
    weights = jnp.where(allowed[:, None, :], jnp.exp(scores), 0.0)
    weight_sum = jnp.sum(weights, axis=-1)
    summed = jnp.einsum(
        "qhk,khd->qhd",
        weights.astype(jnp.bfloat16),
        value_heads,
        preferred_element_type=jnp.float32,
    )
    return (summed.reshape(row_count, model_width), weight_sum)


def shards_columns(
    hidden_in,
    w_qkv,
    w_out,
    w_gate_up,
    w_down,
    scale_qk,
    scale_gate_up,
    eigen_rates,
    cache_keys,
    cache_values,
    page_table,
    request_group,
    suffix_len,
):
    slot_count, model_width = hidden_in.shape
    head_dim = model_width // HEADS
    score_scale = 1.0 / math.sqrt(head_dim)
    mp_count = lax.axis_size("mp")
    mp_index = lax.axis_index("mp")
    own_rows = slot_count // mp_count
    row_first = mp_index * own_rows
    shard_index = lax.axis_index("pages")
    pages_here, page_len = (cache_keys.shape[0], cache_keys.shape[1])
    pool_pages = page_table.shape[0]
    prefix_pages = pool_pages // GROUPS
    slot_valid, request, offset, group_id = slot_tables(suffix_len, request_group, slot_count)
    live_shard = lax.dynamic_index_in_dim(slot_valid, shard_index, 0, keepdims=False)
    request_shard = lax.dynamic_index_in_dim(request, shard_index, 0, keepdims=False)
    offset_shard = lax.dynamic_index_in_dim(offset, shard_index, 0, keepdims=False)
    position_shard = prefix_pages * page_len + offset_shard
    live_own = lax.dynamic_slice_in_dim(live_shard, row_first, own_rows, 0)
    request_own = lax.dynamic_slice_in_dim(request_shard, row_first, own_rows, 0)
    offset_own = lax.dynamic_slice_in_dim(offset_shard, row_first, own_rows, 0)
    position_own = lax.dynamic_slice_in_dim(position_shard, row_first, own_rows, 0)
    state_in = rms_rows(hidden_in.astype(jnp.float32)).astype(jnp.bfloat16)
    projected = jnp.einsum(
        "sd,jdc->jsc", state_in, w_qkv, preferred_element_type=jnp.float32
    ).astype(jnp.bfloat16)
    columns = lax.all_gather(projected, "mp", axis=2, tiled=True)
    query_raw = lax.dynamic_slice_in_dim(columns[0], row_first, own_rows, 0)
    key_raw, value_rows = (columns[1], columns[2])
    queries = head_norm(
        rotate(query_raw.astype(jnp.float32), position_own, HEADS), scale_qk, HEADS
    ).astype(jnp.bfloat16)
    keys_new = head_norm(
        rotate(key_raw.astype(jnp.float32), position_shard, HEADS), scale_qk, HEADS
    ).astype(jnp.bfloat16)
    query_heads = queries.reshape(own_rows, HEADS, head_dim)
    scores = (
        jnp.einsum(
            "qhd,khd->hqk",
            query_heads,
            keys_new.reshape(slot_count, HEADS, head_dim),
            preferred_element_type=jnp.float32,
        )
        * score_scale
    )
    allowed = (
        (request_own[:, None] == request_shard[None, :])
        & (offset_shard[None, :] <= offset_own[:, None])
        & live_own[:, None]
        & live_shard[None, :]
    )
    weights = jnp.where(allowed[None], jnp.exp(scores), 0.0)
    suffix_total = jnp.sum(weights, axis=-1)
    suffix_sum = jnp.einsum(
        "hqk,khd->qhd",
        weights.astype(jnp.bfloat16),
        value_rows.reshape(slot_count, HEADS, head_dim),
        preferred_element_type=jnp.float32,
    )
    physical = shard_index * pages_here + jnp.arange(pages_here, dtype=jnp.int32)
    matches = page_table[:, None] == physical[None, :]
    logical = jnp.sum(
        jnp.where(matches, jnp.arange(pool_pages, dtype=jnp.int32)[:, None], 0), axis=0
    )
    key_group = jnp.repeat(logical // prefix_pages, page_len)
    prefix_keys = head_norm(
        cache_keys.reshape(pages_here * page_len, model_width).astype(jnp.float32), scale_qk, HEADS
    ).astype(jnp.bfloat16)
    prefix_values = cache_values.reshape(pages_here * page_len, model_width)
    gathered = lax.all_gather(queries, "pages", axis=0, tiled=True)
    gathered_group = lax.dynamic_slice_in_dim(group_id, row_first, own_rows, 1).reshape(-1)
    row_count = own_rows * lax.axis_size("pages")
    block_rows = row_count if row_count <= 512 else math.gcd(row_count, 512)

    def attend_block(block_first):
        query_block = lax.dynamic_slice_in_dim(gathered, block_first, block_rows, 0)
        group_block = lax.dynamic_slice_in_dim(gathered_group, block_first, block_rows, 0)
        return prefix_block(
            query_block, group_block, prefix_keys, prefix_values, key_group, score_scale
        )

    block_starts = jnp.arange(row_count // block_rows, dtype=jnp.int32) * block_rows
    summed, weight_sum = lax.map(attend_block, block_starts)
    prefix_sum, prefix_total = lax.psum_scatter(
        (summed.reshape(row_count, model_width), weight_sum.reshape(row_count, HEADS)),
        "pages",
        scatter_dimension=0,
        tiled=True,
    )
    denominator = suffix_total.T + prefix_total + (1.0 - live_own.astype(jnp.float32))[:, None]
    mixed = (suffix_sum + prefix_sum.reshape(own_rows, HEADS, head_dim)) / denominator[:, :, None]
    attention = mixed.reshape(own_rows, model_width).astype(jnp.bfloat16)
    projected_out = jnp.dot(
        lax.all_gather(attention, "mp", axis=0, tiled=True),
        w_out,
        preferred_element_type=jnp.float32,
    )
    residual_in = state_in.astype(jnp.float32)
    state_mid = rms_rows(
        residual_in + eigen_rates[0][None, :] * (rms_rows(projected_out) - residual_in)
    ).astype(jnp.bfloat16)
    state_own = lax.dynamic_slice_in_dim(state_mid, row_first, own_rows, 0)
    gate_up = jnp.einsum("sd,jdf->jsf", state_mid, w_gate_up, preferred_element_type=jnp.float32)
    hidden = (
        jax.nn.silu(scale_gate_up[0][None, :] * gate_up[0])
        * (scale_gate_up[1][None, :] * gate_up[1])
    ).astype(jnp.bfloat16)
    feed_sum = lax.psum_scatter(
        jnp.dot(hidden, w_down, preferred_element_type=jnp.float32),
        "mp",
        scatter_dimension=0,
        tiled=True,
    )
    middle = state_own.astype(jnp.float32)
    result = rms_rows(middle + eigen_rates[1][None, :] * (rms_rows(feed_sum) - middle))
    return (live_own.astype(jnp.float32)[:, None] * result).astype(jnp.bfloat16)


def shards_heads(
    hidden_in,
    w_qkv,
    w_out,
    w_gate_up,
    w_down,
    scale_qk,
    scale_gate_up,
    eigen_rates,
    cache_keys,
    cache_values,
    page_table,
    request_group,
    suffix_len,
):
    slot_count, model_width = hidden_in.shape
    head_dim = model_width // HEADS
    score_scale = 1.0 / math.sqrt(head_dim)
    mp_count = lax.axis_size("mp")
    mp_index = lax.axis_index("mp")
    local_heads = HEADS // mp_count
    local_width = local_heads * head_dim
    own_rows = slot_count // mp_count
    row_first = mp_index * own_rows
    shard_index = lax.axis_index("pages")
    pages_here, page_len = (cache_keys.shape[0], cache_keys.shape[1])
    pool_pages = page_table.shape[0]
    prefix_pages = pool_pages // GROUPS
    slot_valid, request, offset, group_id = slot_tables(suffix_len, request_group, slot_count)
    live_shard = lax.dynamic_index_in_dim(slot_valid, shard_index, 0, keepdims=False)
    request_shard = lax.dynamic_index_in_dim(request, shard_index, 0, keepdims=False)
    offset_shard = lax.dynamic_index_in_dim(offset, shard_index, 0, keepdims=False)
    position_shard = prefix_pages * page_len + offset_shard
    live_own = lax.dynamic_slice_in_dim(live_shard, row_first, own_rows, 0)
    scale_local = lax.dynamic_slice_in_dim(scale_qk, mp_index * local_width, local_width, 0)
    state_in = rms_rows(hidden_in.astype(jnp.float32)).astype(jnp.bfloat16)
    projected = jnp.einsum(
        "sd,jdc->jsc", state_in, w_qkv, preferred_element_type=jnp.float32
    ).astype(jnp.bfloat16)
    queries = head_norm(
        rotate(projected[0].astype(jnp.float32), position_shard, local_heads),
        scale_local,
        local_heads,
    ).astype(jnp.bfloat16)
    keys_new = head_norm(
        rotate(projected[1].astype(jnp.float32), position_shard, local_heads),
        scale_local,
        local_heads,
    ).astype(jnp.bfloat16)
    value_rows = projected[2]
    gathered = lax.all_gather(queries, "pages", axis=0, tiled=True)
    scores = (
        jnp.einsum(
            "qhd,khd->hqk",
            queries.reshape(slot_count, local_heads, head_dim),
            keys_new.reshape(slot_count, local_heads, head_dim),
            preferred_element_type=jnp.float32,
        )
        * score_scale
    )
    allowed = (
        (request_shard[:, None] == request_shard[None, :])
        & (offset_shard[None, :] <= offset_shard[:, None])
        & live_shard[:, None]
        & live_shard[None, :]
    )
    weights = jnp.where(allowed[None], jnp.exp(scores), 0.0)
    suffix_total = jnp.sum(weights, axis=-1)
    suffix_sum = jnp.einsum(
        "hqk,khd->qhd",
        weights.astype(jnp.bfloat16),
        value_rows.reshape(slot_count, local_heads, head_dim),
        preferred_element_type=jnp.float32,
    )
    physical = shard_index * pages_here + jnp.arange(pages_here, dtype=jnp.int32)
    matches = page_table[:, None] == physical[None, :]
    logical = jnp.sum(
        jnp.where(matches, jnp.arange(pool_pages, dtype=jnp.int32)[:, None], 0), axis=0
    )
    key_group = jnp.repeat(logical // prefix_pages, page_len)
    cache_local = lax.dynamic_slice_in_dim(cache_keys, mp_index * local_width, local_width, 2)
    prefix_keys = head_norm(
        cache_local.reshape(pages_here * page_len, local_width).astype(jnp.float32),
        scale_local,
        local_heads,
    ).astype(jnp.bfloat16)
    prefix_values = lax.dynamic_slice_in_dim(
        cache_values, mp_index * local_width, local_width, 2
    ).reshape(pages_here * page_len, local_width)
    gathered_group = group_id.reshape(-1)
    row_count = gathered.shape[0]
    query_heads = gathered.reshape(row_count, local_heads, head_dim)
    key_heads = prefix_keys.reshape(-1, local_heads, head_dim)
    value_heads = prefix_values.reshape(-1, local_heads, head_dim)
    prefix_scores = (
        jnp.einsum("qhd,khd->qhk", query_heads, key_heads, preferred_element_type=jnp.float32)
        * score_scale
    )
    prefix_allowed = gathered_group[:, None] == key_group[None, :]
    prefix_weights = jnp.where(prefix_allowed[:, None, :], jnp.exp(prefix_scores), 0.0)
    weight_sum = jnp.sum(prefix_weights, axis=-1)
    summed = jnp.einsum(
        "qhk,khd->qhd",
        prefix_weights.astype(jnp.bfloat16),
        value_heads,
        preferred_element_type=jnp.float32,
    )
    prefix_sum, prefix_total = lax.psum_scatter(
        (summed.reshape(row_count, local_width), weight_sum),
        "pages",
        scatter_dimension=0,
        tiled=True,
    )
    denominator = suffix_total.T + prefix_total + (1.0 - live_shard.astype(jnp.float32))[:, None]
    mixed = (suffix_sum + prefix_sum.reshape(slot_count, local_heads, head_dim)) / denominator[
        :, :, None
    ]
    attention_local = mixed.reshape(slot_count, local_width).astype(jnp.bfloat16)
    attention = lax.all_gather(attention_local, "mp", axis=1, tiled=True)
    projected_out = jnp.dot(attention, w_out, preferred_element_type=jnp.float32)
    residual_in = state_in.astype(jnp.float32)
    state_mid = rms_rows(
        residual_in + eigen_rates[0][None, :] * (rms_rows(projected_out) - residual_in)
    ).astype(jnp.bfloat16)
    state_own = lax.dynamic_slice_in_dim(state_mid, row_first, own_rows, 0)
    gate_up = jnp.einsum("sd,jdf->jsf", state_mid, w_gate_up, preferred_element_type=jnp.float32)
    hidden = (
        jax.nn.silu(scale_gate_up[0][None, :] * gate_up[0])
        * (scale_gate_up[1][None, :] * gate_up[1])
    ).astype(jnp.bfloat16)
    feed_sum = lax.psum_scatter(
        jnp.dot(hidden, w_down, preferred_element_type=jnp.float32),
        "mp",
        scatter_dimension=0,
        tiled=True,
    )
    middle = state_own.astype(jnp.float32)
    result = rms_rows(middle + eigen_rates[1][None, :] * (rms_rows(feed_sum) - middle))
    return (live_own.astype(jnp.float32)[:, None] * result).astype(jnp.bfloat16)


def solution(mesh):
    shards = shards_heads if HEADS % mesh.shape["mp"] == 0 else shards_columns
    return jax.shard_map(
        shards,
        mesh=mesh,
        in_specs=(
            P("pages", None),
            P(None, None, "mp"),
            P(),
            P(None, None, "mp"),
            P("mp", None),
            P(),
            P(None, "mp"),
            P(),
            P("pages", None, None),
            P("pages", None, None),
            P(),
            P(),
            P(),
        ),
        out_specs=P(("pages", "mp"), None),
        check_vma=False,
    )
```

profile of v0, /device:TPU:0, one launch (start us, length us, event | category | flops | bytes accessed | tf_op | source)
XLA Modules:
  0.0 206.2 jit_solution(12084083910439738020)
XLA Ops:
  9.0 1.3 fusion.9
  10.3 2.8 %fusion.16 = bf16[3,256,320]{1,2,0:T(8,128)(2,1)S(1)} fusion(bf16[3,1280,320]{1,2,0:T(8,128)(2,1)} %param.14, bf16[256,1280]{1,0:T(8,128)(2,1)} %param.13, f32[256]{0:T(256)S(1)} %add_rsqrt_fusion.5), kind=kOutput, calls=%fused_computation.29 | convolution fusion | flops 630374400 | bytes 3605504 | tf_op jit(solution)/shard_map/sd,jdc->jsc/dot_general | solution.py:252
  16.4 1.7 fusion.30
  18.4 2.4 %constant_dynamic-slice_fusion = (bf16[4,128,320]{2,1,0:T(8,128)(2,1)}, bf16[4,128,320]{2,1,0:T(8,128)(2,1)}) fusion(bf16[4,128,1280]{2,1,0:T(8,128)(2,1)} %param.21, s32[]{:T(128)S(6)} %select_n.65, bf16[4,128,1280]{2,1,0:T(8,128)(2,1)} %param.22), kind=kLoop, calls=%fused_computation.90 | loop fusion | bytes 1310724 | tf_op jit(solution)/shard_map/dynamic_slice | solution.py:296
  20.9 1.9 copy.39
  22.8 2.1 copy.35
  24.9 2.2 %reshape.336 = f32[512,5,64]{0,2,1:T(8,128)} reshape(f32[4,128,320]{1,0,2:T(4,128)} %copy.35) | data formatting | bytes 1310720 | tf_op jit(solution)/shard_map/convert_element_type | solution.py:298
  27.1 1.9 copy.33
  29.0 1.9 reshape_reshape.3
  31.0 1.2 multiply_reduce_fusion.2
  32.3 1.6 broadcast_compare_fusion
  33.9 11.8 %all-gather.2.cloned.1.call-done = bf16[2048,320]{0,1:T(8,128)(2,1)} async-done(((bf16[256,320]{0,1:T(8,128)(2,1)}), bf16[2048,320]{0,1:T(8,128)(2,1)}) %all-gather.2.cloned.1.call-update) | async-done | bytes 1310736 | tf_op jit(solution)/shard_map/all_gather | solution.py:266
  45.8 11.8 %fusion = (f32[2048,5]{0,1:T(8,128)}, f32[5,512,2048]{2,1,0:T(8,128)}) fusion(pred[2048,512]{0,1:T(8,128)(4,1)} %broadcast_compare_fusion, bf16[2048,5,64]{0,2,1:T(8,128)(2,1)} %bitcast.93, f32[512,5,64]{0,2,1:T(8,128)} %reshape.336, f32[5,64]{1,0:T(8,128)S(1)} %mul.315, f32[512,5]{0,1:T(8,128)S(1)} %add_rsqrt_fusion), kind=kOutput, calls=%fused_computation.1 | convolution fusion | flops 687298560 | bytes 24038656 | tf_op jit(solution)/shard_map/qhd,khd->qhk/dot_general | solution.py:311
  57.6 12.5 %fusion.2 = f32[5,64,2048]{2,1,0:T(8,128)} fusion(bf16[512,5,64]{0,2,1:T(8,128)(2,1)} %reshape_reshape.3, f32[5,512,2048]{2,1,0:T(8,128)} %get-tuple-element.24, pred[2048,512]{0,1:T(8,128)(4,1)} %broadcast_compare_fusion), kind=kOutput, calls=%fused_computation.3 | convolution fusion | flops 686817280 | bytes 24969216 | tf_op jit(solution)/shard_map/qhk,khd->qhd/dot_general | solution.py:317
  71.5 2.4 %fusion.47 = (f32[5,256]{1,0:T(8,128)S(1)}, bf16[5,256,256]{1,2,0:T(8,128)(2,1)}) fusion(f32[256,5,32]{0,2,1:T(8,128)} %get-tuple-element.16, f32[256,5,32]{0,2,1:T(8,128)S(1)} %get-tuple-element.15, f32[256,5]{0,1:T(8,128)S(1)} %add_rsqrt_fusion.1, f32[5,64]{1,0:T(8,128)S(1)} %mul.315, f32[256,5,64]{0,2,1:T(8,128)} %fusion.33, ...), kind=kOutput, calls=%fused_computation.115 | convolution fusion | flops 43744000 | bytes 1387776 | tf_op jit(solution)/shard_map/qhd,khd->hqk/dot_general | solution.py:268
  73.9 17.0 %reduce-scatter.6.cloned.1.call-done = f32[256,5]{0,1:T(8,128)} async-done(((f32[2048,5]{0,1:T(8,128)}), f32[256,5]{0,1:T(8,128)}) %reduce-scatter.6.cloned.1.call-update) | async-done | bytes 5136 | tf_op jit(solution)/shard_map/reduce_scatter | solution.py:323
  91.6 46.7 %reduce-scatter.4.cloned.1.call-done = f32[256,320]{0,1:T(8,128)} async-done(((f32[2048,320]{0,1:T(8,128)}), f32[256,320]{0,1:T(8,128)}) %reduce-scatter.4.cloned.1.call-update) | async-done | bytes 327696 | tf_op jit(solution)/shard_map/reduce_scatter | solution.py:323
  138.3 1.6 fusion.19
  140.0 18.1 %all_gather.7 = bf16[256,1280]{0,1:T(8,128)(2,1)S(1)} all-gather(bf16[256,320]{0,1:T(8,128)(2,1)S(1)} %bitcast.87), channel_id=1, replica_groups=mesh['pages'=8,'mp'=4] {'mp'}, dimensions={1}, use_global_device_ids=true | all-gather | bytes 819200 | tf_op jit(solution)/shard_map/all_gather | solution.py:334
  160.2 1.9 convolution_bitcast_fusion
  162.3 2.3 %fusion.20 = f32[256,1280]{1,0:T(8,128)} fusion(bf16[1280,1280]{1,0:T(8,128)(2,1)S(1)} %copy-done.5, f32[2,256,1280]{2,1,0:T(8,128)S(1)} %convolution_bitcast_fusion, f32[1280]{0:T(1024)S(1)} %get-tuple-element.8, f32[1280]{0:T(1024)S(1)} %get-tuple-element.7), kind=kOutput, calls=%fused_computation.34 | convolution fusion | flops 841482240 | bytes 7219200 | tf_op jit(solution)/shard_map/dot_general | solution.py:347
  164.7 30.6 %reduce-scatter.8.cloned.1.call-done = f32[64,1280]{1,0:T(8,128)} async-done(((f32[256,1280]{1,0:T(8,128)}), f32[64,1280]{1,0:T(8,128)}) %reduce-scatter.8.cloned.1.call-update) | async-done | bytes 327696 | tf_op jit(solution)/shard_map/reduce_scatter | solution.py:346
  196.4 1.3 multiply_reduce_fusion.3
  197.7 1.9 multiply_convert_fusion.3
  (69 shorter events, 11.8 us)
Async XLA Ops:
  6.5 151.5 %copy-start = (bf16[1280,1280]{1,0:T(8,128)(2,1)S(1)}, bf16[1280,1280]{1,0:T(8,128)(2,1)}, u32[]{:S(2)}) copy-start(bf16[1280,1280]{1,0:T(8,128)(2,1)} %param.15) | copy-start | bytes 9830404
  6.5 39.2 %all-gather.2.cloned.1.call-start = ((), (), s32[]{:S(2)}) async-start(), calls=%async_computation.3 | async-start | bytes 1474560 | tf_op jit(solution)/shard_map/all_gather | solution.py:266
  18.2 72.7 %reduce-scatter.6.cloned.1.call-start = ((), (), s32[]{:S(2)}) async-start(), calls=%async_computation.5 | async-start | bytes 73728 | tf_op jit(solution)/shard_map/reduce_scatter | solution.py:323
  24.9 6.0 %copy-start.6 = (s32[32]{0:T(128)S(1)}, s32[32]{0:T(128)}, u32[]{:S(2)}) copy-start(s32[32]{0:T(128)} %param.23) | copy-start | bytes 388
  57.6 80.8 %reduce-scatter.4.cloned.1.call-start = ((), (), s32[]{:S(2)}) async-start(), calls=%async_computation.4 | async-start | bytes 2949120 | tf_op jit(solution)/shard_map/reduce_scatter | solution.py:323
  70.1 1.1 copy-start.3
  70.1 1.1 copy-start.4
  70.1 125.2 %reduce-scatter.8.cloned.1.call-start = ((), (), s32[]{:S(2)}) async-start(), calls=%async_computation.6 | async-start | bytes 1638400 | tf_op jit(solution)/shard_map/reduce_scatter | solution.py:346
  138.3 21.8 %slice-start = ((s8[6553600]{0:T(1024)(128)(4,1)}), s8[4194304]{0:T(1024)(128)(4,1)S(1)}, s32[]{:S(2)}) async-start(s8[6553600]{0:T(1024)(128)(4,1)} %bitcast.82), calls=%async_computation.7 | async-start | bytes 8388608
  158.0 1.1 copy-start.1
  158.0 2.1 %slice-start.1 = ((s8[6553600]{0:T(1024)(128)(4,1)}), s8[2359296]{0:T(1024)(128)(4,1)S(1)}, s32[]{:S(2)}) async-start(s8[6553600]{0:T(1024)(128)(4,1)} %bitcast.82), calls=%async_computation.8 | async-start | bytes 4718592
  160.1 1.9 copy-start.2
  160.2 2.2 %copy-start.5 = (bf16[1280,1280]{1,0:T(8,128)(2,1)S(1)}, bf16[1280,1280]{1,0:T(8,128)(2,1)}, u32[]{:S(2)}) copy-start(bf16[1280,1280]{1,0:T(8,128)(2,1)} %param.17) | copy-start | bytes 9830404
Sparse Core Ops, SparseCore 0:
  18.3 27.4 all-gather.1
  57.7 33.2 reduce-scatter.5
  94.6 43.6 reduce-scatter.3
  164.8 30.4 reduce-scatter.7
where the time goes:
time: 207 us; the launch traced here: 206 us
  waiting for transfers between devices  106 us (51%)
  matrix products  36.4 us (18%)
  blocking collectives  18.1 us (9%)
  other arithmetic  17.5 us (8%)
  local copies, waits for them, and re-layouts  14.4 us (7%)
  between operations  13.4 us (6%)
    reduce_scatter x2, waiting for transfers between devices, shards_heads(): lax.psum_scatter((summed.reshape(row_count, local_width), weight_sum), 'p...  63.7 us
    reduce_scatter x1, waiting for transfers between devices, shards_heads(): lax.psum_scatter(jnp.dot(hidden, w_down, preferred_element_type=jnp.float...  30.6 us
    all_gather x1, blocking collectives, shards_heads(): attention = lax.all_gather(attention_local, 'mp', axis=1, tiled=True)  18.1 us
    dot_general x1, matrix products, shards_heads(): jnp.einsum('qhk,khd->qhd', prefix_weights.astype(jnp.bfloat16), value_hea...  12.5 us
    all_gather x1, waiting for transfers between devices, shards_heads(): gathered = lax.all_gather(queries, 'pages', axis=0, tiled=True)  11.8 us
    dot_general x1, matrix products, shards_heads(): jnp.einsum('qhd,khd->qhk', query_heads, key_heads, preferred_element_type...  11.8 us
    convert_element_type x2, local copies, waits for them, and re-layouts, shards_heads(): cache_local.reshape(pages_here * page_len, local_width).astype(jnp.float32)  4.28 us
    reduce_sum x4, other arithmetic, rms_rows(): jnp.mean(values_in * values_in, axis=-1, keepdims=True) + EPSILON  4.16 us
  transfers between devices with their start and end apart: 4, of which 4 were waited for; matrix products, arithmetic and copies ran while one was open for 16% of the time, Pallas kernels for 0%

commit v1 on v0

--- a/solution.py
+++ b/solution.py
@@ -263,7 +263,14 @@
         local_heads,
     ).astype(jnp.bfloat16)
     value_rows = projected[2]
-    gathered = lax.all_gather(queries, "pages", axis=0, tiled=True)
+    n_dev = lax.axis_size("pages")
+    forward = [(i, (i + 1) % n_dev) for i in range(n_dev)]
+    shards_2 = [queries]
+    for stride in range(1, n_dev):
+        shards_2 = [lax.ppermute(shards_2[0], "pages", forward), *shards_2]
+    whole = jnp.concatenate(shards_2, axis=0)
+    places = (lax.axis_index("pages") + 1) * shards_2[-1].shape[0]
+    gathered = jnp.roll(whole, places, axis=0)
     scores = (
         jnp.einsum(
             "qhd,khd->hqk",

time: 207 us -> 239 us (1.15)
  waiting for transfers between devices: 106 us -> 127 us
  local copies, waits for them, and re-layouts: 14.4 us -> 25.8 us
    ppermute x0 -> x7, waiting for transfers between devices: none -> 32.7 us  [shards_heads(): shards_2 = [lax.ppermute(shards_2[0], 'pages', forward), *shards_2]]
    all_gather x1 -> x0, waiting for transfers between devices: 11.8 us -> none  [shards_heads(): gathered = lax.all_gather(queries, 'pages', axis=0, tiled=True)]
    unnamed x20 -> x53, local copies, waits for them, and re-layouts: 2.24 us -> 13.4 us
  transfers between devices with their start and end apart: 4 -> 10, of which waited for: 4 -> 9; matrix products, arithmetic and copies ran while one was open for 16% -> 14% of each run, Pallas kernels for 0% -> 0%
where the time goes in v1:
time: 239 us; the launch traced here: 238 us
  waiting for transfers between devices  127 us (53%)
  matrix products  35.4 us (15%)
  local copies, waits for them, and re-layouts  25.8 us (11%)
  blocking collectives  17.9 us (7%)
  other arithmetic  17 us (7%)
  between operations  13.6 us (6%)
    reduce_scatter x2, waiting for transfers between devices, shards_heads(): lax.psum_scatter((summed.reshape(row_count, local_width), weight_sum), 'p...  63.8 us
    ppermute x7, waiting for transfers between devices, shards_heads(): shards_2 = [lax.ppermute(shards_2[0], 'pages', forward), *shards_2]  32.7 us
    reduce_scatter x1, waiting for transfers between devices, shards_heads(): lax.psum_scatter(jnp.dot(hidden, w_down, preferred_element_type=jnp.float...  30.6 us
    all_gather x1, blocking collectives, shards_heads(): attention = lax.all_gather(attention_local, 'mp', axis=1, tiled=True)  17.9 us
    unnamed x53, local copies, waits for them, and re-layouts  13.4 us
    dot_general x1, matrix products, shards_heads(): jnp.einsum('qhk,khd->qhd', prefix_weights.astype(jnp.bfloat16), value_hea...  12.5 us
    dot_general x1, matrix products, shards_heads(): jnp.einsum('qhd,khd->qhk', query_heads, key_heads, preferred_element_type...  10.8 us
  transfers between devices with their start and end apart: 10, of which 9 were waited for; matrix products, arithmetic and copies ran while one was open for 14% of the time, Pallas kernels for 0%

profile of v1, /device:TPU:0, one launch (start us, length us, event | category | flops | bytes accessed | tf_op | source)
XLA Modules:
  0.0 237.6 jit_solution(2204304393689355294)
XLA Ops:
  10.3 2.8 %fusion.16 = bf16[3,256,320]{1,2,0:T(8,128)(2,1)S(1)} fusion(bf16[3,1280,320]{1,2,0:T(8,128)(2,1)} %param.14, bf16[256,1280]{1,0:T(8,128)(2,1)} %param.13, f32[256]{0:T(256)S(1)} %add_rsqrt_fusion.5), kind=kOutput, calls=%fused_computation.29 | convolution fusion | flops 630374400 | bytes 3605504 | tf_op jit(solution)/shard_map/sd,jdc->jsc/dot_general | solution.py:252
  18.2 5.9 %collective-permute-done = bf16[256,320]{0,1:T(8,128)(2,1)} collective-permute-done((bf16[256,320]{0,1:T(8,128)(2,1)S(1)}, bf16[256,320]{0,1:T(8,128)(2,1)}, u32[]{:S(2)}, u32[]{:S(2)}) %collective-permute-start) | collective-permute-done | bytes 163872 | tf_op jit(solution)/shard_map/ppermute | solution.py:270
  24.3 5.6 %collective-permute-done.1 = bf16[256,320]{0,1:T(8,128)(2,1)S(1)} collective-permute-done((bf16[256,320]{0,1:T(8,128)(2,1)}, bf16[256,320]{0,1:T(8,128)(2,1)S(1)}, u32[]{:S(2)}, u32[]{:S(2)}) %collective-permute-start.1) | collective-permute-done | bytes 163872 | tf_op jit(solution)/shard_map/ppermute | solution.py:270
  30.7 5.6 %collective-permute-done.2 = bf16[256,320]{0,1:T(8,128)(2,1)S(1)} collective-permute-done((bf16[256,320]{0,1:T(8,128)(2,1)S(1)}, bf16[256,320]{0,1:T(8,128)(2,1)S(1)}, u32[]{:S(2)}, u32[]{:S(2)}) %collective-permute-start.2) | collective-permute-done | bytes 163872 | tf_op jit(solution)/shard_map/ppermute | solution.py:270
  37.0 5.6 %collective-permute-done.3 = bf16[256,320]{0,1:T(8,128)(2,1)S(1)} collective-permute-done((bf16[256,320]{0,1:T(8,128)(2,1)S(1)}, bf16[256,320]{0,1:T(8,128)(2,1)S(1)}, u32[]{:S(2)}, u32[]{:S(2)}) %collective-permute-start.3) | collective-permute-done | bytes 163872 | tf_op jit(solution)/shard_map/ppermute | solution.py:270
  43.3 1.6 broadcast_compare_fusion
  44.9 4.1 %collective-permute-done.4 = bf16[256,320]{0,1:T(8,128)(2,1)} collective-permute-done((bf16[256,320]{0,1:T(8,128)(2,1)S(1)}, bf16[256,320]{0,1:T(8,128)(2,1)}, u32[]{:S(2)}, u32[]{:S(2)}) %collective-permute-start.4) | collective-permute-done | bytes 163872 | tf_op jit(solution)/shard_map/ppermute | solution.py:270
  49.0 2.4 %constant_dynamic-slice_fusion.1 = (bf16[4,128,320]{2,1,0:T(8,128)(2,1)}, bf16[4,128,320]{2,1,0:T(8,128)(2,1)}) fusion(bf16[4,128,1280]{2,1,0:T(8,128)(2,1)} %param.21, s32[]{:T(128)S(6)} %select_n.78, bf16[4,128,1280]{2,1,0:T(8,128)(2,1)} %param.22), kind=kLoop, calls=%fused_computation.107 | loop fusion | bytes 1310724 | tf_op jit(solution)/shard_map/dynamic_slice | solution.py:303
  51.5 1.9 copy.39
  53.4 2.1 copy.35
  55.5 2.2 reshape.336
  57.7 1.9 copy.33
  59.6 1.9 reshape_reshape.3
  62.8 5.8 %collective-permute-done.6 = bf16[256,320]{0,1:T(8,128)(2,1)S(1)} collective-permute-done((bf16[256,320]{0,1:T(8,128)(2,1)}, bf16[256,320]{0,1:T(8,128)(2,1)S(1)}, u32[]{:S(2)}, u32[]{:S(2)}) %collective-permute-start.6) | collective-permute-done | bytes 163872 | tf_op jit(solution)/shard_map/ppermute | solution.py:270
  77.5 10.8 %fusion = (f32[2048,5]{0,1:T(8,128)}, f32[5,512,2048]{2,1,0:T(8,128)}) fusion(pred[2048,512]{0,1:T(8,128)(4,1)S(1)} %copy-done.3, bf16[2048,5,64]{0,2,1:T(8,128)(2,1)S(1)} %bitcast.85, f32[512,5,64]{0,2,1:T(8,128)S(1)} %copy-done.4, f32[5,64]{1,0:T(8,128)S(1)} %mul.318, f32[512,5]{0,1:T(8,128)S(1)} %add_rsqrt_fusion), kind=kOutput, calls=%fused_computation.1 | convolution fusion | flops 687298560 | bytes 24038656 | tf_op jit(solution)/shard_map/qhd,khd->qhk/dot_general | solution.py:318
  88.3 12.5 %fusion.2 = f32[5,64,2048]{2,1,0:T(8,128)} fusion(bf16[512,5,64]{0,2,1:T(8,128)(2,1)} %reshape_reshape.3, f32[5,512,2048]{2,1,0:T(8,128)} %get-tuple-element.24, pred[2048,512]{0,1:T(8,128)(4,1)} %broadcast_compare_fusion), kind=kOutput, calls=%fused_computation.3 | convolution fusion | flops 686817280 | bytes 24969216 | tf_op jit(solution)/shard_map/qhk,khd->qhd/dot_general | solution.py:324
  103.0 2.4 %fusion.47 = (f32[5,256]{1,0:T(8,128)S(1)}, bf16[5,256,256]{1,2,0:T(8,128)(2,1)}) fusion(f32[256,5,32]{0,2,1:T(8,128)} %get-tuple-element.16, f32[256,5,32]{0,2,1:T(8,128)S(1)} %copy-done.11, f32[256,5]{0,1:T(8,128)S(1)} %add_rsqrt_fusion.1, f32[5,64]{1,0:T(8,128)S(1)} %mul.318, f32[256,5,64]{0,2,1:T(8,128)} %fusion.33, pred[256,256]{0,1:T(8,128)(4,1)S(1)} %and_and_fusion), kind=kOutput, calls=%fused_computation.132 | convolution fusion | flops 43744000 | bytes 1387776 | tf_op jit(solution)/shard_map/qhd,khd->hqk/dot_general | solution.py:275
  105.4 17.2 %reduce-scatter.6.cloned.1.call-done = f32[256,5]{0,1:T(8,128)} async-done(((f32[2048,5]{0,1:T(8,128)}), f32[256,5]{0,1:T(8,128)}) %reduce-scatter.6.cloned.1.call-update) | async-done | bytes 5136 | tf_op jit(solution)/shard_map/reduce_scatter | solution.py:330
  123.3 46.7 %reduce-scatter.4.cloned.1.call-done = f32[256,320]{0,1:T(8,128)} async-done(((f32[2048,320]{0,1:T(8,128)}), f32[256,320]{0,1:T(8,128)}) %reduce-scatter.4.cloned.1.call-update) | async-done | bytes 327696 | tf_op jit(solution)/shard_map/reduce_scatter | solution.py:330
  171.6 17.9 %all_gather.3 = bf16[256,1280]{0,1:T(8,128)(2,1)S(1)} all-gather(bf16[256,320]{0,1:T(8,128)(2,1)S(1)} %bitcast.88), channel_id=1, replica_groups=mesh['pages'=8,'mp'=4] {'mp'}, dimensions={1}, use_global_device_ids=true | all-gather | bytes 819200 | tf_op jit(solution)/shard_map/all_gather | solution.py:341
  191.6 1.9 convolution_bitcast_fusion
  193.8 2.3 fusion.20
  196.2 30.6 %reduce-scatter.8.cloned.1.call-done = f32[64,1280]{1,0:T(8,128)} async-done(((f32[256,1280]{1,0:T(8,128)}), f32[64,1280]{1,0:T(8,128)}) %reduce-scatter.8.cloned.1.call-update) | async-done | bytes 327696 | tf_op jit(solution)/shard_map/reduce_scatter | solution.py:353
  229.2 1.9 multiply_convert_fusion.3
  (115 shorter events, 30.5 us)
Async XLA Ops:
  6.5 183.0 %copy-start = (bf16[1280,1280]{1,0:T(8,128)(2,1)S(1)}, bf16[1280,1280]{1,0:T(8,128)(2,1)}, u32[]{:S(2)}) copy-start(bf16[1280,1280]{1,0:T(8,128)(2,1)} %param.15) | copy-start | bytes 9830404
  6.5 116.1 %reduce-scatter.6.cloned.1.call-start = ((), (), s32[]{:S(2)}) async-start(), calls=%async_computation.4 | async-start | bytes 73728 | tf_op jit(solution)/shard_map/reduce_scatter | solution.py:330
  13.2 11.0 %copy-start.15 = (s32[32]{0:T(128)S(1)}, s32[32]{0:T(128)}, u32[]{:S(2)}) copy-start(s32[32]{0:T(128)} %param.23) | copy-start | bytes 388
  17.6 6.5 %collective-permute-start = (bf16[256,320]{0,1:T(8,128)(2,1)S(1)}, bf16[256,320]{0,1:T(8,128)(2,1)}, u32[]{:S(2)}, u32[]{:S(2)}) collective-permute-start(bf16[256,320]{0,1:T(8,128)(2,1)S(1)} %fusion.30), channel_id=1, source_target_pairs={{0,4},{4,8},{8,12},{12,16},{16,20},{20,24},{24,28},{28,0},{1,5},{5... | collective-permute-start | bytes 491528 | tf_op jit(solution)/shard_map/ppermute | solution.py:270
  24.1 5.9 %collective-permute-start.1 = (bf16[256,320]{0,1:T(8,128)(2,1)}, bf16[256,320]{0,1:T(8,128)(2,1)S(1)}, u32[]{:S(2)}, u32[]{:S(2)}) collective-permute-start(bf16[256,320]{0,1:T(8,128)(2,1)} %collective-permute-done), channel_id=1, source_target_pairs={{0,4},{4,8},{8,12},{12,16},{16,20},{20,24},{24,28},{28,0},{1,5},{5... | collective-permute-start | bytes 491528 | tf_op jit(solution)/shard_map/ppermute | solution.py:270
  30.7 5.6 %collective-permute-start.2 = (bf16[256,320]{0,1:T(8,128)(2,1)S(1)}, bf16[256,320]{0,1:T(8,128)(2,1)S(1)}, u32[]{:S(2)}, u32[]{:S(2)}) collective-permute-start(bf16[256,320]{0,1:T(8,128)(2,1)S(1)} %collective-permute-done.1), channel_id=1, source_target_pairs={{0,4},{4,8},{8,12},{12,16},{16,20},{20,24},{24,28},{28,0},{1,5},{5... | collective-permute-start | bytes 491528 | tf_op jit(solution)/shard_map/ppermute | solution.py:270
  37.0 5.6 %collective-permute-start.3 = (bf16[256,320]{0,1:T(8,128)(2,1)S(1)}, bf16[256,320]{0,1:T(8,128)(2,1)S(1)}, u32[]{:S(2)}, u32[]{:S(2)}) collective-permute-start(bf16[256,320]{0,1:T(8,128)(2,1)S(1)} %collective-permute-done.2), channel_id=1, source_target_pairs={{0,4},{4,8},{8,12},{12,16},{16,20},{20,24},{24,28},{28,0},{1,5},{5... | collective-permute-start | bytes 491528 | tf_op jit(solution)/shard_map/ppermute | solution.py:270
  43.3 5.7 %collective-permute-start.4 = (bf16[256,320]{0,1:T(8,128)(2,1)S(1)}, bf16[256,320]{0,1:T(8,128)(2,1)}, u32[]{:S(2)}, u32[]{:S(2)}) collective-permute-start(bf16[256,320]{0,1:T(8,128)(2,1)S(1)} %collective-permute-done.3), channel_id=1, source_target_pairs={{0,4},{4,8},{8,12},{12,16},{16,20},{20,24},{24,28},{28,0},{1,5},{5... | collective-permute-start | bytes 491528 | tf_op jit(solution)/shard_map/ppermute | solution.py:270
  49.0 13.7 %collective-permute-start.5 = (bf16[256,320]{0,1:T(8,128)(2,1)}, bf16[256,320]{0,1:T(8,128)(2,1)}, u32[]{:S(2)}, u32[]{:S(2)}) collective-permute-start(bf16[256,320]{0,1:T(8,128)(2,1)} %collective-permute-done.4), channel_id=1, source_target_pairs={{0,4},{4,8},{8,12},{12,16},{16,20},{20,24},{24,28},{28,0},{1,5},{5... | collective-permute-start | bytes 491528 | tf_op jit(solution)/shard_map/ppermute | solution.py:270
  61.4 14.8 %copy-start.10 = (bf16[256,320]{0,1:T(8,128)(2,1)S(1)}, bf16[256,320]{0,1:T(8,128)(2,1)}, u32[]{:S(2)}) copy-start(bf16[256,320]{0,1:T(8,128)(2,1)} %copy-done.9) | copy-start | bytes 491524
  61.4 14.9 %copy-start.8 = (bf16[256,320]{0,1:T(8,128)(2,1)S(1)}, bf16[256,320]{0,1:T(8,128)(2,1)}, u32[]{:S(2)}) copy-start(bf16[256,320]{0,1:T(8,128)(2,1)} %copy-done.7) | copy-start | bytes 491524
  61.5 14.9 %copy-start.6 = (bf16[256,320]{0,1:T(8,128)(2,1)S(1)}, bf16[256,320]{0,1:T(8,128)(2,1)}, u32[]{:S(2)}) copy-start(bf16[256,320]{0,1:T(8,128)(2,1)} %copy-done.5) | copy-start | bytes 491524
  62.7 5.9 %collective-permute-start.6 = (bf16[256,320]{0,1:T(8,128)(2,1)}, bf16[256,320]{0,1:T(8,128)(2,1)S(1)}, u32[]{:S(2)}, u32[]{:S(2)}) collective-permute-start(bf16[256,320]{0,1:T(8,128)(2,1)} %collective-permute-done.5), channel_id=1, source_target_pairs={{0,4},{4,8},{8,12},{12,16},{16,20},{20,24},{24,28},{28,0},{1,5},{5... | collective-permute-start | bytes 491528 | tf_op jit(solution)/shard_map/ppermute | solution.py:270
  74.3 3.2 %copy-start.3 = (pred[2048,512]{0,1:T(8,128)(4,1)S(1)}, pred[2048,512]{0,1:T(8,128)(4,1)}, u32[]{:S(2)}) copy-start(pred[2048,512]{0,1:T(8,128)(4,1)} %broadcast_compare_fusion) | copy-start | bytes 3145732
  74.3 3.2 %copy-start.4 = (f32[512,5,64]{0,2,1:T(8,128)S(1)}, f32[512,5,64]{0,2,1:T(8,128)}, u32[]{:S(2)}) copy-start(f32[512,5,64]{0,2,1:T(8,128)} %reshape.336) | copy-start | bytes 1966084
  88.3 81.7 %reduce-scatter.4.cloned.1.call-start = ((), (), s32[]{:S(2)}) async-start(), calls=%async_computation.3 | async-start | bytes 2949120 | tf_op jit(solution)/shard_map/reduce_scatter | solution.py:330
  100.8 1.9 copy-start.12
  100.8 1.9 copy-start.13
  100.8 125.9 %reduce-scatter.8.cloned.1.call-start = ((), (), s32[]{:S(2)}) async-start(), calls=%async_computation.5 | async-start | bytes 1638400 | tf_op jit(solution)/shard_map/reduce_scatter | solution.py:353
  170.0 21.6 %slice-start = ((s8[6553600]{0:T(1024)(128)(4,1)}), s8[4194304]{0:T(1024)(128)(4,1)S(1)}, s32[]{:S(2)}) async-start(s8[6553600]{0:T(1024)(128)(4,1)} %bitcast.82), calls=%async_computation.6 | async-start | bytes 8388608
  189.5 1.1 copy-start.1
  189.5 2.1 slice-start.1
  191.6 1.9 copy-start.2
  191.6 2.2 copy-start.14
  (4 other events, 2.9 us)
Sparse Core Ops, SparseCore 0:
  88.4 34.1 reduce-scatter.5
  126.3 43.6 reduce-scatter.3
  196.2 30.4 reduce-scatter.7
